TPU v7x, 256 devices: a whole 4x4x8 slice. The times are simulated.
256 devices in a mesh: grp: 4 (over x_lo, core), gx: 16 (over z, x_hi), gy: 4 (over y).
Axes of the slice: x: 4 (x_hi: 2, x_lo: 2; x = x_hi * 2 + x_lo), y: 4, z: 8, core: 2. Of those that a mesh axis runs over, the one named last changes fastest.
Arguments:
- conc: float32 [4, 32, 1024, 1024], P('grp', None, 'gx', 'gy'), may hold values from 0 to 1
- velocity: bfloat16 [3, 4, 32, 1024, 1024], P(None, 'grp', None, 'gx', 'gy'), may hold values from -0.119628906 to 0.119628906
- porosity: bfloat16 [4, 32, 1024, 1024], P('grp', None, 'gx', 'gy'), may hold values from 0.099609375 to 0.3984375
- saturation: bfloat16 [4, 32, 1024, 1024], P('grp', None, 'gx', 'gy'), may hold values from 0.29882812 to 1
- layer_counts: int32 [8], replicated, may hold values from 1 to 24, 96 in all
- electrodes: int32 [4, 2], replicated, may hold values from 0 to 2097151
- init_potential: float32 [4, 8, 512, 512], P(None, None, 'gx', 'gy'), may hold values from -6 to 6
Outputs:
- conc_next: float32 [4, 32, 1024, 1024], P('grp', None, 'gx', 'gy')
- conductivity: float32 [8, 512, 512], P(None, 'gx', 'gy')
- potential: float32 [4, 8, 512, 512], P('grp', None, 'gx', 'gy')
Inputs may be any that keep to these rules, and one draw needn't show every extreme that they name: layer_counts sums to 96; its largest entry is exactly 24.
All inputs are finite; a program needn't handle non-finite values.
Results may differ from a plain program's by a relative error of at most 0.0014.
Values may be sent and summed in bfloat16 or wider, within the bound.
No kernel may reach another device: no remote copies, remote signals or barrier semaphores. Data moves between devices by JAX's collectives and lax.ppermute only.
A program may use at most 128 MiB of HBM per device.

v0:
```python
import jax
import jax.numpy as jnp
from jax import lax
from jax.sharding import PartitionSpec as P

SWEEPS = 3
KAPPA = 0.06
OMEGA = 0.8
AMPLITUDE = 40.0
ARCHIE = 20.0


def with_halo(shard, sides, width):
    for axis, dim in sides:
        devices, length = (lax.axis_size(axis), shard.shape[dim])
        up = [(i, (i + 1) % devices) for i in range(devices - 1)]
        down = [(j, i) for i, j in up]
        last = lax.slice_in_dim(shard, length - width, length, axis=dim)
        initial = lax.slice_in_dim(shard, 0, width, axis=dim)
        before = lax.ppermute(last, axis, up)
        after = lax.ppermute(initial, axis, down)
        shard = jnp.concatenate([before, shard, after], axis=dim)
    return shard


def neighbours(padded, direction_index):
    leading = [slice(None)] * (padded.ndim - 3)
    middle = [slice(1, -1)] * 3
    below_slices = list(middle)
    below_slices[direction_index] = slice(0, -2)
    above_slices = list(middle)
    above_slices[direction_index] = slice(2, None)
    return (padded[tuple(leading + below_slices)], padded[tuple(leading + above_slices)])


def tendency(padded, speeds):
    center = padded[1:-1, 1:-1, 1:-1]
    running = -6.0 * KAPPA * center
    for direction_index in range(3):
        below_cells, above_cells = neighbours(padded, direction_index)
        speed_comp = speeds[direction_index]
        running = (
            running
            + KAPPA * (below_cells + above_cells)
            - (
                jnp.maximum(speed_comp, 0.0) * (center - below_cells)
                + jnp.minimum(speed_comp, 0.0) * (above_cells - center)
            )
        )
    return running


def section_halo(values):
    return with_halo(values, (("grp", 0), ("gx", 1), ("gy", 2)), 1)


def potential_halo(values):
    return with_halo(values, (("gx", 2), ("gy", 3)), 1)


def face_terms(cond_padded, center):
    faces = []
    diagonal = jnp.zeros_like(center)
    for direction_index in range(3):
        below_cells, above_cells = neighbours(cond_padded, direction_index)
        face_below = 0.5 * (center + below_cells)
        face_above = 0.5 * (center + above_cells)
        faces.append((face_below, face_above))
        diagonal = diagonal + face_below + face_above
    return (faces, diagonal)


def sweep_once(potential, faces, diagonal, source_terms, pot_wide):
    coupled = jnp.zeros_like(potential)
    for direction_index in range(3):
        below_cells, above_cells = neighbours(pot_wide, direction_index)
        coupled = (
            coupled
            + faces[direction_index][0] * below_cells
            + faces[direction_index][1] * above_cells
        )
    applied = diagonal * potential - coupled
    return potential + OMEGA * (source_terms - applied) / diagonal


def on_device(conc, velocity, porosity, saturation, layer_counts, electrodes, init_potential):
    group_index = lax.axis_index("grp")
    row_index = lax.axis_index("gx")
    column_index = lax.axis_index("gy")
    active = group_index < 3
    field = jnp.where(active, conc[0], 0.0)
    speeds = velocity[:, 0].astype(jnp.float32)
    layers, tile_x, tile_y = field.shape
    section_one = jnp.where(active, field + tendency(section_halo(field), speeds), 0.0)
    advanced = 0.5 * (field + section_one + tendency(section_halo(section_one), speeds))
    advanced = jnp.where(active, advanced, 0.0)
    poro = porosity[0].astype(jnp.float32)
    water = saturation[0].astype(jnp.float32)
    sigma = ARCHIE * jnp.exp(advanced) * poro * poro * water * water
    coarse_x = tile_x // 2
    coarse_y = tile_y // 2
    coarse = sigma.reshape(layers, coarse_x, 2, coarse_y, 2).sum(axis=(2, 4))
    ends = jnp.cumsum(layer_counts)
    starts = ends - layer_counts
    layer_ids = group_index * layers + jnp.arange(layers, dtype=jnp.int32)
    member = (
        (layer_ids[None, :] >= starts[:, None]) & (layer_ids[None, :] < ends[:, None]) & active
    ).astype(jnp.float32)
    weights = member / (4.0 * layer_counts.astype(jnp.float32))[:, None]
    resist_layers = layer_counts.shape[0]
    partial_cond = jnp.dot(
        weights, coarse.reshape(layers, coarse_x * coarse_y), precision=lax.Precision.HIGHEST
    ).reshape(resist_layers, coarse_x, coarse_y)
    conductivity = lax.psum(partial_cond, "grp")
    grid_x = coarse_x * lax.axis_size("gx")
    grid_y = coarse_y * lax.axis_size("gy")
    potential = lax.dynamic_slice_in_dim(init_potential, group_index, 1, 0)
    poles = lax.dynamic_slice_in_dim(electrodes, group_index, 1, 0)
    cond_padded = jnp.pad(
        with_halo(conductivity, (("gx", 1), ("gy", 2)), 1), ((1, 1), (0, 0), (0, 0))
    )
    faces, diagonal = face_terms(cond_padded, conductivity)
    flat_ids = (
        jnp.arange(resist_layers, dtype=jnp.int32)[:, None, None] * (grid_x * grid_y)
        + (row_index * coarse_x + jnp.arange(coarse_x, dtype=jnp.int32))[None, :, None] * grid_y
        + (column_index * coarse_y + jnp.arange(coarse_y, dtype=jnp.int32))[None, None, :]
    )
    source_terms = AMPLITUDE * (
        (flat_ids[None] == poles[:, 0, None, None, None]).astype(jnp.float32)
        - (flat_ids[None] == poles[:, 1, None, None, None]).astype(jnp.float32)
    )
    for sweep_index in range(SWEEPS):
        pot_wide = jnp.pad(potential_halo(potential), ((0, 0), (1, 1), (0, 0), (0, 0)))
        potential = sweep_once(potential, faces, diagonal, source_terms, pot_wide)
    return (advanced[None], conductivity, potential)


def solution(mesh):
    in_specs = (
        P("grp", None, "gx", "gy"),
        P(None, "grp", None, "gx", "gy"),
        P("grp", None, "gx", "gy"),
        P("grp", None, "gx", "gy"),
        P(),
        P(),
        P(None, None, "gx", "gy"),
    )
    out_specs = (P("grp", None, "gx", "gy"), P(None, "gx", "gy"), P("grp", None, "gx", "gy"))
    return jax.shard_map(
        on_device, mesh=mesh, in_specs=in_specs, out_specs=out_specs, check_vma=False
    )
```

profile of v0, /device:TPU:70, one launch (start us, length us, event | category | flops | bytes accessed | tf_op | source)
XLA Modules:
  0.0 272.3 jit_solution(4352050345593786454)
XLA Ops:
  7.2 1.8 broadcast_select_fusion
  9.0 1.9 collective-permute-start
  11.0 3.6 %collective-permute-start.1 = (f32[1,64,256]{2,1,0:T(8,128)S(1)}, f32[1,64,256]{2,1,0:T(8,128)S(1)}, u32[]{:S(2)}, u32[]{:S(2)}) collective-permute-start(f32[1,64,256]{2,1,0:T(8,128)S(1)} %get-tuple-element.28), channel_id=1, source_target_pairs={{64,0},{128,64},{192,128},{65,1},{129,65},{193,129},{66,2},{130,66... | collective-permute-start | bytes 196616 | tf_op jit(solution)/shard_map/ppermute | solution.py:21
  15.3 4.7 %collective-permute-start.16 = (f32[1,8,1,128]{3,1,2,0:T(8,128)S(1)}, f32[1,8,1,128]{3,1,2,0:T(8,128)S(1)}, u32[]{:S(2)}, u32[]{:S(2)}) collective-permute-start(f32[1,8,1,128]{3,1,2,0:T(8,128)S(1)} %get-tuple-element.44), channel_id=1, source_target_pairs={{0,4},{4,8},{8,12},{12,16},{16,20},{20,24},{24,28},{28,32},{32,36}... | collective-permute-start | bytes 12296 | tf_op jit(solution)/shard_map/ppermute | solution.py:20
  20.0 2.7 collective-permute-start.17
  22.7 1.8 fusion.129
  26.8 5.6 %collective-permute-start.2 = (f32[34,1,256]{2,1,0:T(1,128)S(1)}, f32[34,1,256]{2,1,0:T(1,128)S(1)}, u32[]{:S(2)}, u32[]{:S(2)}) collective-permute-start(f32[34,1,256]{2,1,0:T(1,128)S(1)} %get-tuple-element.23), channel_id=1, source_target_pairs={{0,4},{4,8},{8,12},{12,16},{16,20},{20,24},{24,28},{28,32},{32,36}... | collective-permute-start | bytes 104456 | tf_op jit(solution)/shard_map/ppermute | solution.py:20
  32.4 1.9 collective-permute-start.3
  34.4 6.2 %collective-permute-done.3 = f32[34,1,256]{2,1,0:T(1,128)S(1)} collective-permute-done((f32[34,1,256]{2,1,0:T(1,128)S(1)}, f32[34,1,256]{2,1,0:T(1,128)S(1)}, u32[]{:S(2)}, u32[]{:S(2)}) %collective-permute-start.3) | collective-permute-done | bytes 34848 | tf_op jit(solution)/shard_map/ppermute | solution.py:21
  40.9 1.8 fusion.118
  42.8 1.8 copy.29
  44.6 3.5 %collective-permute-start.4 = (f32[34,66,1]{1,2,0:T(1,128)S(1)}, f32[34,66,1]{1,2,0:T(1,128)S(1)}, u32[]{:S(2)}, u32[]{:S(2)}) collective-permute-start(f32[34,66,1]{1,2,0:T(1,128)S(1)} %copy.29), channel_id=1, source_target_pairs={{0,1},{1,2},{2,3},{4,5},{5,6},{6,7},{8,9},{9,10},{10,11},{12,13},{... | collective-permute-start | bytes 26936 | tf_op jit(solution)/shard_map/ppermute | solution.py:20
  50.5 5.5 %convert_element_type.50 = f32[3,1,32,64,256]{4,3,2,1,0:T(8,128)} convert(bf16[3,1,32,64,256]{4,3,2,1,0:T(8,128)(2,1)} %param.8) | non-fusion elementwise | flops 1572864 | bytes 9437184 | tf_op jit(solution)/shard_map/convert_element_type | solution.py:92
  59.1 14.5 %fusion.31 = f32[32,64,256]{2,1,0:T(8,128)S(1)} fusion(f32[32,64,256]{2,1,0:T(8,128)} %copy-done.1, f32[34,1,256]{2,1,0:T(1,128)S(1)} %collective-permute-done.3, f32[1,64,256]{2,1,0:T(8,128)S(1)} %collective-permute-done.1, f32[1,64,256]{2,1,0:T(8,128)S(1)} %collective-permute-done, f32[34,1,256]{2,1,0:T(1,128)S(1)} %collective-permute-done.2, ...), kind=kLoop, calls=%fused_computation.66 | loop fusion | flops 28311552 | bytes 10704417 | tf_op jit(solution)/shard_map/jit(_where)/select_n | solution.py:94
  73.6 1.9 collective-permute-start.6
  75.6 3.6 %collective-permute-start.7 = (f32[1,64,256]{2,1,0:T(8,128)S(1)}, f32[1,64,256]{2,1,0:T(8,128)S(1)}, u32[]{:S(2)}, u32[]{:S(2)}) collective-permute-start(f32[1,64,256]{2,1,0:T(8,128)S(1)} %get-tuple-element.26), channel_id=1, source_target_pairs={{64,0},{128,64},{192,128},{65,1},{129,65},{193,129},{66,2},{130,66... | collective-permute-start | bytes 196616 | tf_op jit(solution)/shard_map/ppermute | solution.py:21
  81.2 4.8 %collective-permute-start.8 = (f32[34,1,256]{2,1,0:T(1,128)S(1)}, f32[34,1,256]{2,1,0:T(1,128)S(1)}, u32[]{:S(2)}, u32[]{:S(2)}) collective-permute-start(f32[34,1,256]{2,1,0:T(1,128)S(1)} %get-tuple-element.21), channel_id=1, source_target_pairs={{0,4},{4,8},{8,12},{12,16},{16,20},{20,24},{24,28},{28,32},{32,36}... | collective-permute-start | bytes 104456 | tf_op jit(solution)/shard_map/ppermute | solution.py:20
  86.0 2.5 collective-permute-start.9
  89.1 6.3 %collective-permute-done.9 = f32[34,1,256]{2,1,0:T(1,128)S(1)} collective-permute-done((f32[34,1,256]{2,1,0:T(1,128)S(1)}, f32[34,1,256]{2,1,0:T(1,128)S(1)}, u32[]{:S(2)}, u32[]{:S(2)}) %collective-permute-start.9) | collective-permute-done | bytes 34848 | tf_op jit(solution)/shard_map/ppermute | solution.py:21
  95.7 1.8 fusion.117
  97.6 1.7 copy.33
  99.3 4.6 %collective-permute-start.10 = (f32[34,66,1]{1,2,0:T(1,128)S(1)}, f32[34,66,1]{1,2,0:T(1,128)S(1)}, u32[]{:S(2)}, u32[]{:S(2)}) collective-permute-start(f32[34,66,1]{1,2,0:T(1,128)S(1)} %copy.33), channel_id=1, source_target_pairs={{0,1},{1,2},{2,3},{4,5},{5,6},{6,7},{8,9},{9,10},{10,11},{12,13},{... | collective-permute-start | bytes 26936 | tf_op jit(solution)/shard_map/ppermute | solution.py:20
  103.9 1.7 copy.35
  108.7 2.6 collective-permute-done.11
  112.8 11.8 %multiply_multiply_fusion = (f32[32,64,256]{2,1,0:T(8,128)}, f32[32,64,256]{2,1,0:T(8,128)}) fusion(bf16[1,32,64,256]{3,2,1,0:T(8,128)(2,1)} %param.10, bf16[1,32,64,256]{3,2,1,0:T(8,128)(2,1)} %param.9, f32[32,64,256]{2,1,0:T(8,128)S(1)} %fusion.31, f32[3,1,32,64,256]{4,3,2,1,0:T(8,128)} %convert_element_type.50, f32[34,66,1]{2,1,0:T(8,128)} %copy.36, ...), kind=kLoop, calls=%fused_computation | loop fusion | flops 33554432 | bytes 16996896 | tf_op jit(solution)/shard_map/mul | solution.py:99
  124.7 6.4 %copy.37 = f32[32,64,256]{0,2,1:T(8,128)} copy(f32[32,64,256]{2,1,0:T(8,128)} %get-tuple-element.15) | data formatting | bytes 4194304 | tf_op jit(solution)/shard_map/mul | solution.py:99
  131.0 9.5 %reduce_sum.9 = f32[32,32,128]{0,2,1:T(8,128)S(1)} reduce(f32[32,32,2,128,2]{0,4,3,2,1:T(2,128)} %bitcast.106, f32[]{:T(128)} %constant.8.clone.1), dimensions={2,4}, to_apply=%region_1.2 | reduce | flops 393216 | bytes 2621444 | tf_op jit(solution)/shard_map/reduce_sum | solution.py:102
  141.2 1.7 fusion.49
  143.0 40.0 %all-reduce.6.cloned.1.call-done = f32[8,32,128]{2,0,1:T(8,128)} async-done(((f32[8,32,128]{2,0,1:T(8,128)}), f32[8,32,128]{2,0,1:T(8,128)}) %all-reduce.6.cloned.1.call-update) | async-done | bytes 131088 | tf_op jit(solution)/shard_map/psum | solution.py:114
  183.8 4.1 %collective-permute-start.12 = (f32[8,1,128]{2,0,1:T(8,128)S(1)}, f32[8,1,128]{2,0,1:T(8,128)S(1)}, u32[]{:S(2)}, u32[]{:S(2)}) collective-permute-start(f32[8,1,128]{2,0,1:T(8,128)S(1)} %get-tuple-element.42), channel_id=1, source_target_pairs={{0,4},{4,8},{8,12},{12,16},{16,20},{20,24},{24,28},{28,32},{32,36}... | collective-permute-start | bytes 12296 | tf_op jit(solution)/shard_map/ppermute | solution.py:20
  188.0 3.4 %collective-permute-start.18 = (f32[1,8,34,1]{3,1,2,0:T(8,128)S(1)}, f32[1,8,34,1]{3,1,2,0:T(8,128)S(1)}, u32[]{:S(2)}, u32[]{:S(2)}) collective-permute-start(f32[1,8,34,1]{3,1,2,0:T(8,128)S(1)} %get-tuple-element.35), channel_id=1, source_target_pairs={{0,1},{1,2},{2,3},{4,5},{5,6},{6,7},{8,9},{9,10},{10,11},{12,13},{... | collective-permute-start | bytes 3272 | tf_op jit(solution)/shard_map/ppermute | solution.py:20
  192.7 3.2 %collective-permute-start.13 = (f32[8,1,128]{2,0,1:T(8,128)S(1)}, f32[8,1,128]{2,0,1:T(8,128)S(1)}, u32[]{:S(2)}, u32[]{:S(2)}) collective-permute-start(f32[8,1,128]{2,0,1:T(8,128)S(1)} %get-tuple-element.41), channel_id=1, source_target_pairs={{4,0},{8,4},{12,8},{16,12},{20,16},{24,20},{28,24},{32,28},{36,32}... | collective-permute-start | bytes 12296 | tf_op jit(solution)/shard_map/ppermute | solution.py:21
  196.9 3.7 %collective-permute-done.13 = f32[8,1,128]{2,0,1:T(8,128)S(1)} collective-permute-done((f32[8,1,128]{2,0,1:T(8,128)S(1)}, f32[8,1,128]{2,0,1:T(8,128)S(1)}, u32[]{:S(2)}, u32[]{:S(2)}) %collective-permute-start.13) | collective-permute-done | bytes 4128 | tf_op jit(solution)/shard_map/ppermute | solution.py:21
  200.7 4.6 %collective-permute-start.14 = (f32[8,34,1]{2,0,1:T(8,128)S(1)}, f32[8,34,1]{2,0,1:T(8,128)S(1)}, u32[]{:S(2)}, u32[]{:S(2)}) collective-permute-start(f32[8,34,1]{2,0,1:T(8,128)S(1)} %get-tuple-element.33), channel_id=1, source_target_pairs={{0,1},{1,2},{2,3},{4,5},{5,6},{6,7},{8,9},{9,10},{10,11},{12,13},{... | collective-permute-start | bytes 3272 | tf_op jit(solution)/shard_map/ppermute | solution.py:20
  207.8 4.4 %collective-permute-done.15 = f32[8,34,1]{2,0,1:T(8,128)S(1)} collective-permute-done((f32[8,34,1]{2,0,1:T(8,128)S(1)}, f32[8,34,1]{2,0,1:T(8,128)S(1)}, u32[]{:S(2)}, u32[]{:S(2)}) %collective-permute-start.15) | collective-permute-done | bytes 1120 | tf_op jit(solution)/shard_map/ppermute | solution.py:21
  212.5 1.8 fusion.86
  214.3 3.3 %collective-permute-start.20 = (f32[1,8,1,128]{3,1,2,0:T(8,128)S(1)}, f32[1,8,1,128]{3,1,2,0:T(8,128)S(1)}, u32[]{:S(2)}, u32[]{:S(2)}) collective-permute-start(f32[1,8,1,128]{3,1,2,0:T(8,128)S(1)} %get-tuple-element.39), channel_id=1, source_target_pairs={{0,4},{4,8},{8,12},{12,16},{16,20},{20,24},{24,28},{28,32},{32,36}... | collective-permute-start | bytes 12296 | tf_op jit(solution)/shard_map/ppermute | solution.py:20
  217.7 4.0 %collective-permute-start.21 = (f32[1,8,1,128]{3,1,2,0:T(8,128)S(1)}, f32[1,8,1,128]{3,1,2,0:T(8,128)S(1)}, u32[]{:S(2)}, u32[]{:S(2)}) collective-permute-start(f32[1,8,1,128]{3,1,2,0:T(8,128)S(1)} %get-tuple-element.40), channel_id=1, source_target_pairs={{4,0},{8,4},{12,8},{16,12},{20,16},{24,20},{28,24},{32,28},{36,32}... | collective-permute-start | bytes 12296 | tf_op jit(solution)/shard_map/ppermute | solution.py:21
  221.7 5.0 %collective-permute-done.21 = f32[1,8,1,128]{3,1,2,0:T(8,128)S(1)} collective-permute-done((f32[1,8,1,128]{3,1,2,0:T(8,128)S(1)}, f32[1,8,1,128]{3,1,2,0:T(8,128)S(1)}, u32[]{:S(2)}, u32[]{:S(2)}) %collective-permute-start.21) | collective-permute-done | bytes 4128 | tf_op jit(solution)/shard_map/ppermute | solution.py:21
  226.8 3.4 %collective-permute-start.22 = (f32[1,8,34,1]{3,1,2,0:T(8,128)S(1)}, f32[1,8,34,1]{3,1,2,0:T(8,128)S(1)}, u32[]{:S(2)}, u32[]{:S(2)}) collective-permute-start(f32[1,8,34,1]{3,1,2,0:T(8,128)S(1)} %get-tuple-element.31), channel_id=1, source_target_pairs={{0,1},{1,2},{2,3},{4,5},{5,6},{6,7},{8,9},{9,10},{10,11},{12,13},{... | collective-permute-start | bytes 3272 | tf_op jit(solution)/shard_map/ppermute | solution.py:20
  232.8 4.4 %collective-permute-done.23 = f32[1,8,34,1]{3,1,2,0:T(8,128)S(1)} collective-permute-done((f32[1,8,34,1]{3,1,2,0:T(8,128)S(1)}, f32[1,8,34,1]{3,1,2,0:T(8,128)S(1)}, u32[]{:S(2)}, u32[]{:S(2)}) %collective-permute-start.23) | collective-permute-done | bytes 1120 | tf_op jit(solution)/shard_map/ppermute | solution.py:21
  237.4 1.8 fusion.72
  239.2 5.4 %collective-permute-start.24 = (f32[1,8,1,128]{3,1,2,0:T(8,128)S(1)}, f32[1,8,1,128]{3,1,2,0:T(8,128)S(1)}, u32[]{:S(2)}, u32[]{:S(2)}) collective-permute-start(f32[1,8,1,128]{3,1,2,0:T(8,128)S(1)} %get-tuple-element.37), channel_id=1, source_target_pairs={{0,4},{4,8},{8,12},{12,16},{16,20},{20,24},{24,28},{28,32},{32,36}... | collective-permute-start | bytes 12296 | tf_op jit(solution)/shard_map/ppermute | solution.py:20
  244.7 1.9 collective-permute-start.25
  246.6 6.0 %collective-permute-done.25 = f32[1,8,1,128]{3,1,2,0:T(8,128)S(1)} collective-permute-done((f32[1,8,1,128]{3,1,2,0:T(8,128)S(1)}, f32[1,8,1,128]{3,1,2,0:T(8,128)S(1)}, u32[]{:S(2)}, u32[]{:S(2)}) %collective-permute-start.25) | collective-permute-done | bytes 4128 | tf_op jit(solution)/shard_map/ppermute | solution.py:21
  252.7 3.1 %collective-permute-start.26 = (f32[1,8,34,1]{3,1,2,0:T(8,128)S(1)}, f32[1,8,34,1]{3,1,2,0:T(8,128)S(1)}, u32[]{:S(2)}, u32[]{:S(2)}) collective-permute-start(f32[1,8,34,1]{3,1,2,0:T(8,128)S(1)} %get-tuple-element.29), channel_id=1, source_target_pairs={{0,1},{1,2},{2,3},{4,5},{5,6},{6,7},{8,9},{9,10},{10,11},{12,13},{... | collective-permute-start | bytes 3272 | tf_op jit(solution)/shard_map/ppermute | solution.py:20
  258.4 4.4 %collective-permute-done.27 = f32[1,8,34,1]{3,1,2,0:T(8,128)S(1)} collective-permute-done((f32[1,8,34,1]{3,1,2,0:T(8,128)S(1)}, f32[1,8,34,1]{3,1,2,0:T(8,128)S(1)}, u32[]{:S(2)}, u32[]{:S(2)}) %collective-permute-start.27) | collective-permute-done | bytes 1120 | tf_op jit(solution)/shard_map/ppermute | solution.py:21
  263.0 1.8 fusion.58
  (91 shorter events, 29.7 us)
Async XLA Ops:
  7.2 7.5 %copy-start = (f32[4,8,32,128]{3,2,1,0:T(8,128)S(1)}, f32[4,8,32,128]{3,2,1,0:T(8,128)}, u32[]{:S(2)}) copy-start(f32[4,8,32,128]{3,2,1,0:T(8,128)} %param.13) | copy-start | bytes 1572868
  7.2 175.8 %all-reduce.6.cloned.1.call-start = ((), (), s32[]{:S(2)}) async-start(), calls=%async_computation | async-start | bytes 262144 | tf_op jit(solution)/shard_map/psum | solution.py:114
  9.0 17.7 %collective-permute-start = (f32[1,64,256]{2,1,0:T(8,128)S(1)}, f32[1,64,256]{2,1,0:T(8,128)S(1)}, u32[]{:S(2)}, u32[]{:S(2)}) collective-permute-start(f32[1,64,256]{2,1,0:T(8,128)S(1)} %get-tuple-element.27), channel_id=1, source_target_pairs={{0,64},{64,128},{128,192},{1,65},{65,129},{129,193},{2,66},{66,130... | collective-permute-start | bytes 196616 | tf_op jit(solution)/shard_map/ppermute | solution.py:20
  11.0 15.8 %collective-permute-start.1 = (f32[1,64,256]{2,1,0:T(8,128)S(1)}, f32[1,64,256]{2,1,0:T(8,128)S(1)}, u32[]{:S(2)}, u32[]{:S(2)}) collective-permute-start(f32[1,64,256]{2,1,0:T(8,128)S(1)} %get-tuple-element.28), channel_id=1, source_target_pairs={{64,0},{128,64},{192,128},{65,1},{129,65},{193,129},{66,2},{130,66... | collective-permute-start | bytes 196616 | tf_op jit(solution)/shard_map/ppermute | solution.py:21
  15.3 91.8 %collective-permute-start.16 = (f32[1,8,1,128]{3,1,2,0:T(8,128)S(1)}, f32[1,8,1,128]{3,1,2,0:T(8,128)S(1)}, u32[]{:S(2)}, u32[]{:S(2)}) collective-permute-start(f32[1,8,1,128]{3,1,2,0:T(8,128)S(1)} %get-tuple-element.44), channel_id=1, source_target_pairs={{0,4},{4,8},{8,12},{12,16},{16,20},{20,24},{24,28},{28,32},{32,36}... | collective-permute-start | bytes 12296 | tf_op jit(solution)/shard_map/ppermute | solution.py:20
  20.0 4.5 %copy-start.8 = (s32[8]{0:T(128)S(1)}, s32[8]{0:T(128)}, u32[]{:S(2)}) copy-start(s32[8]{0:T(128)} %param.11) | copy-start | bytes 100
  20.0 123.0 %collective-permute-start.17 = (f32[1,8,1,128]{3,1,2,0:T(8,128)}, f32[1,8,1,128]{3,1,2,0:T(8,128)S(1)}, u32[]{:S(2)}, u32[]{:S(2)}) collective-permute-start(f32[1,8,1,128]{3,1,2,0:T(8,128)} %get-tuple-element.43), channel_id=1, source_target_pairs={{4,0},{8,4},{12,8},{16,12},{20,16},{24,20},{28,24},{32,28},{36,32}... | collective-permute-start | bytes 12296 | tf_op jit(solution)/shard_map/ppermute | solution.py:21
  24.5 16.4 %copy-start.1 = (f32[32,64,256]{2,1,0:T(8,128)}, f32[32,64,256]{2,1,0:T(8,128)S(1)}, u32[]{:S(2)}) copy-start(f32[32,64,256]{2,1,0:T(8,128)S(1)} %fusion.129) | copy-start | bytes 6291460
  24.5 9.8 %copy-start.6 = (s32[4,2]{0,1:T(2,128)S(1)}, s32[4,2]{0,1:T(2,128)}, u32[]{:S(2)}) copy-start(s32[4,2]{0,1:T(2,128)} %param.12) | copy-start | bytes 100
  24.7 0.8 copy-start.7
  26.8 7.6 %collective-permute-start.2 = (f32[34,1,256]{2,1,0:T(1,128)S(1)}, f32[34,1,256]{2,1,0:T(1,128)S(1)}, u32[]{:S(2)}, u32[]{:S(2)}) collective-permute-start(f32[34,1,256]{2,1,0:T(1,128)S(1)} %get-tuple-element.23), channel_id=1, source_target_pairs={{0,4},{4,8},{8,12},{12,16},{16,20},{20,24},{24,28},{28,32},{32,36}... | collective-permute-start | bytes 104456 | tf_op jit(solution)/shard_map/ppermute | solution.py:20
  32.4 8.2 %collective-permute-start.3 = (f32[34,1,256]{2,1,0:T(1,128)S(1)}, f32[34,1,256]{2,1,0:T(1,128)S(1)}, u32[]{:S(2)}, u32[]{:S(2)}) collective-permute-start(f32[34,1,256]{2,1,0:T(1,128)S(1)} %get-tuple-element.24), channel_id=1, source_target_pairs={{4,0},{8,4},{12,8},{16,12},{20,16},{24,20},{28,24},{32,28},{36,32}... | collective-permute-start | bytes 104456 | tf_op jit(solution)/shard_map/ppermute | solution.py:21
  42.7 5.3 %copy-start.2 = (f32[34,66,1]{2,1,0:T(8,128)S(1)}, f32[34,66,1]{2,1,0:T(8,128)}, u32[]{:S(2)}) copy-start(f32[34,66,1]{2,1,0:T(8,128)} %get-tuple-element.19) | copy-start | bytes 26932
  44.6 11.3 %collective-permute-start.4 = (f32[34,66,1]{1,2,0:T(1,128)S(1)}, f32[34,66,1]{1,2,0:T(1,128)S(1)}, u32[]{:S(2)}, u32[]{:S(2)}) collective-permute-start(f32[34,66,1]{1,2,0:T(1,128)S(1)} %copy.29), channel_id=1, source_target_pairs={{0,1},{1,2},{2,3},{4,5},{5,6},{6,7},{8,9},{9,10},{10,11},{12,13},{... | collective-permute-start | bytes 26936 | tf_op jit(solution)/shard_map/ppermute | solution.py:20
  48.6 8.9 %collective-permute-start.5 = (f32[34,66,1]{1,2,0:T(1,128)S(1)}, f32[34,66,1]{1,2,0:T(1,128)S(1)}, u32[]{:S(2)}, u32[]{:S(2)}) collective-permute-start(f32[34,66,1]{1,2,0:T(1,128)S(1)} %copy.31), channel_id=1, source_target_pairs={{1,0},{2,1},{3,2},{5,4},{6,5},{7,6},{9,8},{10,9},{11,10},{13,12},{... | collective-permute-start | bytes 26936 | tf_op jit(solution)/shard_map/ppermute | solution.py:21
  73.6 6.1 %collective-permute-start.6 = (f32[1,64,256]{2,1,0:T(8,128)S(1)}, f32[1,64,256]{2,1,0:T(8,128)S(1)}, u32[]{:S(2)}, u32[]{:S(2)}) collective-permute-start(f32[1,64,256]{2,1,0:T(8,128)S(1)} %get-tuple-element.25), channel_id=1, source_target_pairs={{0,64},{64,128},{128,192},{1,65},{65,129},{129,193},{2,66},{66,130... | collective-permute-start | bytes 196616 | tf_op jit(solution)/shard_map/ppermute | solution.py:20
  75.6 5.5 %collective-permute-start.7 = (f32[1,64,256]{2,1,0:T(8,128)S(1)}, f32[1,64,256]{2,1,0:T(8,128)S(1)}, u32[]{:S(2)}, u32[]{:S(2)}) collective-permute-start(f32[1,64,256]{2,1,0:T(8,128)S(1)} %get-tuple-element.26), channel_id=1, source_target_pairs={{64,0},{128,64},{192,128},{65,1},{129,65},{193,129},{66,2},{130,66... | collective-permute-start | bytes 196616 | tf_op jit(solution)/shard_map/ppermute | solution.py:21
  81.2 8.0 %collective-permute-start.8 = (f32[34,1,256]{2,1,0:T(1,128)S(1)}, f32[34,1,256]{2,1,0:T(1,128)S(1)}, u32[]{:S(2)}, u32[]{:S(2)}) collective-permute-start(f32[34,1,256]{2,1,0:T(1,128)S(1)} %get-tuple-element.21), channel_id=1, source_target_pairs={{0,4},{4,8},{8,12},{12,16},{16,20},{20,24},{24,28},{28,32},{32,36}... | collective-permute-start | bytes 104456 | tf_op jit(solution)/shard_map/ppermute | solution.py:20
  86.0 9.4 %collective-permute-start.9 = (f32[34,1,256]{2,1,0:T(1,128)S(1)}, f32[34,1,256]{2,1,0:T(1,128)S(1)}, u32[]{:S(2)}, u32[]{:S(2)}) collective-permute-start(f32[34,1,256]{2,1,0:T(1,128)S(1)} %get-tuple-element.22), channel_id=1, source_target_pairs={{4,0},{8,4},{12,8},{16,12},{20,16},{24,20},{28,24},{32,28},{36,32}... | collective-permute-start | bytes 104456 | tf_op jit(solution)/shard_map/ppermute | solution.py:21
  99.3 7.8 %collective-permute-start.10 = (f32[34,66,1]{1,2,0:T(1,128)S(1)}, f32[34,66,1]{1,2,0:T(1,128)S(1)}, u32[]{:S(2)}, u32[]{:S(2)}) collective-permute-start(f32[34,66,1]{1,2,0:T(1,128)S(1)} %copy.33), channel_id=1, source_target_pairs={{0,1},{1,2},{2,3},{4,5},{5,6},{6,7},{8,9},{9,10},{10,11},{12,13},{... | collective-permute-start | bytes 26936 | tf_op jit(solution)/shard_map/ppermute | solution.py:20
  105.6 5.7 %collective-permute-start.11 = (f32[34,66,1]{1,2,0:T(1,128)S(1)}, f32[34,66,1]{1,2,0:T(1,128)S(1)}, u32[]{:S(2)}, u32[]{:S(2)}) collective-permute-start(f32[34,66,1]{1,2,0:T(1,128)S(1)} %copy.35), channel_id=1, source_target_pairs={{1,0},{2,1},{3,2},{5,4},{6,5},{7,6},{9,8},{10,9},{11,10},{13,12},{... | collective-permute-start | bytes 26936 | tf_op jit(solution)/shard_map/ppermute | solution.py:21
  141.2 71.3 %copy-start.4 = (s32[8,32]{0,1:T(8,128)S(1)}, s32[8,32]{0,1:T(8,128)}, u32[]{:S(2)}) copy-start(s32[8,32]{0,1:T(8,128)} %broadcast_add_fusion) | copy-start | bytes 3076
  141.2 71.4 %copy-start.5 = (s32[128]{0:T(128)S(1)}, s32[128]{0:T(128)}, u32[]{:S(2)}) copy-start(s32[128]{0:T(128)} %iota_add_fusion) | copy-start | bytes 1540
  183.0 29.5 %copy-start.3 = (f32[8,32,128]{2,0,1:T(8,128)S(1)}, f32[8,32,128]{2,0,1:T(8,128)}, u32[]{:S(2)}) copy-start(f32[8,32,128]{2,0,1:T(8,128)} %all-reduce.6.cloned.1.call-done) | copy-start | bytes 393220
  183.8 12.2 %collective-permute-start.12 = (f32[8,1,128]{2,0,1:T(8,128)S(1)}, f32[8,1,128]{2,0,1:T(8,128)S(1)}, u32[]{:S(2)}, u32[]{:S(2)}) collective-permute-start(f32[8,1,128]{2,0,1:T(8,128)S(1)} %get-tuple-element.42), channel_id=1, source_target_pairs={{0,4},{4,8},{8,12},{12,16},{16,20},{20,24},{24,28},{28,32},{32,36}... | collective-permute-start | bytes 12296 | tf_op jit(solution)/shard_map/ppermute | solution.py:20
  188.0 18.6 %collective-permute-start.18 = (f32[1,8,34,1]{3,1,2,0:T(8,128)S(1)}, f32[1,8,34,1]{3,1,2,0:T(8,128)S(1)}, u32[]{:S(2)}, u32[]{:S(2)}) collective-permute-start(f32[1,8,34,1]{3,1,2,0:T(8,128)S(1)} %get-tuple-element.35), channel_id=1, source_target_pairs={{0,1},{1,2},{2,3},{4,5},{5,6},{6,7},{8,9},{9,10},{10,11},{12,13},{... | collective-permute-start | bytes 3272 | tf_op jit(solution)/shard_map/ppermute | solution.py:20
  191.4 15.2 %collective-permute-start.19 = (f32[1,8,34,1]{3,1,2,0:T(8,128)S(1)}, f32[1,8,34,1]{3,1,2,0:T(8,128)S(1)}, u32[]{:S(2)}, u32[]{:S(2)}) collective-permute-start(f32[1,8,34,1]{3,1,2,0:T(8,128)S(1)} %get-tuple-element.36), channel_id=1, source_target_pairs={{1,0},{2,1},{3,2},{5,4},{6,5},{7,6},{9,8},{10,9},{11,10},{13,12},{... | collective-permute-start | bytes 3272 | tf_op jit(solution)/shard_map/ppermute | solution.py:21
  192.7 7.9 %collective-permute-start.13 = (f32[8,1,128]{2,0,1:T(8,128)S(1)}, f32[8,1,128]{2,0,1:T(8,128)S(1)}, u32[]{:S(2)}, u32[]{:S(2)}) collective-permute-start(f32[8,1,128]{2,0,1:T(8,128)S(1)} %get-tuple-element.41), channel_id=1, source_target_pairs={{4,0},{8,4},{12,8},{16,12},{20,16},{24,20},{28,24},{32,28},{36,32}... | collective-permute-start | bytes 12296 | tf_op jit(solution)/shard_map/ppermute | solution.py:21
  200.7 7.1 %collective-permute-start.14 = (f32[8,34,1]{2,0,1:T(8,128)S(1)}, f32[8,34,1]{2,0,1:T(8,128)S(1)}, u32[]{:S(2)}, u32[]{:S(2)}) collective-permute-start(f32[8,34,1]{2,0,1:T(8,128)S(1)} %get-tuple-element.33), channel_id=1, source_target_pairs={{0,1},{1,2},{2,3},{4,5},{5,6},{6,7},{8,9},{9,10},{10,11},{12,13},{... | collective-permute-start | bytes 3272 | tf_op jit(solution)/shard_map/ppermute | solution.py:20
  205.3 6.9 %collective-permute-start.15 = (f32[8,34,1]{2,0,1:T(8,128)S(1)}, f32[8,34,1]{2,0,1:T(8,128)S(1)}, u32[]{:S(2)}, u32[]{:S(2)}) collective-permute-start(f32[8,34,1]{2,0,1:T(8,128)S(1)} %get-tuple-element.34), channel_id=1, source_target_pairs={{1,0},{2,1},{3,2},{5,4},{6,5},{7,6},{9,8},{10,9},{11,10},{13,12},{... | collective-permute-start | bytes 3272 | tf_op jit(solution)/shard_map/ppermute | solution.py:21
  214.3 7.4 %collective-permute-start.20 = (f32[1,8,1,128]{3,1,2,0:T(8,128)S(1)}, f32[1,8,1,128]{3,1,2,0:T(8,128)S(1)}, u32[]{:S(2)}, u32[]{:S(2)}) collective-permute-start(f32[1,8,1,128]{3,1,2,0:T(8,128)S(1)} %get-tuple-element.39), channel_id=1, source_target_pairs={{0,4},{4,8},{8,12},{12,16},{16,20},{20,24},{24,28},{28,32},{32,36}... | collective-permute-start | bytes 12296 | tf_op jit(solution)/shard_map/ppermute | solution.py:20
  217.7 9.0 %collective-permute-start.21 = (f32[1,8,1,128]{3,1,2,0:T(8,128)S(1)}, f32[1,8,1,128]{3,1,2,0:T(8,128)S(1)}, u32[]{:S(2)}, u32[]{:S(2)}) collective-permute-start(f32[1,8,1,128]{3,1,2,0:T(8,128)S(1)} %get-tuple-element.40), channel_id=1, source_target_pairs={{4,0},{8,4},{12,8},{16,12},{20,16},{24,20},{28,24},{32,28},{36,32}... | collective-permute-start | bytes 12296 | tf_op jit(solution)/shard_map/ppermute | solution.py:21
  226.8 6.0 %collective-permute-start.22 = (f32[1,8,34,1]{3,1,2,0:T(8,128)S(1)}, f32[1,8,34,1]{3,1,2,0:T(8,128)S(1)}, u32[]{:S(2)}, u32[]{:S(2)}) collective-permute-start(f32[1,8,34,1]{3,1,2,0:T(8,128)S(1)} %get-tuple-element.31), channel_id=1, source_target_pairs={{0,1},{1,2},{2,3},{4,5},{5,6},{6,7},{8,9},{9,10},{10,11},{12,13},{... | collective-permute-start | bytes 3272 | tf_op jit(solution)/shard_map/ppermute | solution.py:20
  230.2 6.9 %collective-permute-start.23 = (f32[1,8,34,1]{3,1,2,0:T(8,128)S(1)}, f32[1,8,34,1]{3,1,2,0:T(8,128)S(1)}, u32[]{:S(2)}, u32[]{:S(2)}) collective-permute-start(f32[1,8,34,1]{3,1,2,0:T(8,128)S(1)} %get-tuple-element.32), channel_id=1, source_target_pairs={{1,0},{2,1},{3,2},{5,4},{6,5},{7,6},{9,8},{10,9},{11,10},{13,12},{... | collective-permute-start | bytes 3272 | tf_op jit(solution)/shard_map/ppermute | solution.py:21
  239.2 7.4 %collective-permute-start.24 = (f32[1,8,1,128]{3,1,2,0:T(8,128)S(1)}, f32[1,8,1,128]{3,1,2,0:T(8,128)S(1)}, u32[]{:S(2)}, u32[]{:S(2)}) collective-permute-start(f32[1,8,1,128]{3,1,2,0:T(8,128)S(1)} %get-tuple-element.37), channel_id=1, source_target_pairs={{0,4},{4,8},{8,12},{12,16},{16,20},{20,24},{24,28},{28,32},{32,36}... | collective-permute-start | bytes 12296 | tf_op jit(solution)/shard_map/ppermute | solution.py:20
  244.7 7.9 %collective-permute-start.25 = (f32[1,8,1,128]{3,1,2,0:T(8,128)S(1)}, f32[1,8,1,128]{3,1,2,0:T(8,128)S(1)}, u32[]{:S(2)}, u32[]{:S(2)}) collective-permute-start(f32[1,8,1,128]{3,1,2,0:T(8,128)S(1)} %get-tuple-element.38), channel_id=1, source_target_pairs={{4,0},{8,4},{12,8},{16,12},{20,16},{24,20},{28,24},{32,28},{36,32}... | collective-permute-start | bytes 12296 | tf_op jit(solution)/shard_map/ppermute | solution.py:21
  252.7 5.7 %collective-permute-start.26 = (f32[1,8,34,1]{3,1,2,0:T(8,128)S(1)}, f32[1,8,34,1]{3,1,2,0:T(8,128)S(1)}, u32[]{:S(2)}, u32[]{:S(2)}) collective-permute-start(f32[1,8,34,1]{3,1,2,0:T(8,128)S(1)} %get-tuple-element.29), channel_id=1, source_target_pairs={{0,1},{1,2},{2,3},{4,5},{5,6},{6,7},{8,9},{9,10},{10,11},{12,13},{... | collective-permute-start | bytes 3272 | tf_op jit(solution)/shard_map/ppermute | solution.py:20
  255.8 6.9 %collective-permute-start.27 = (f32[1,8,34,1]{3,1,2,0:T(8,128)S(1)}, f32[1,8,34,1]{3,1,2,0:T(8,128)S(1)}, u32[]{:S(2)}, u32[]{:S(2)}) collective-permute-start(f32[1,8,34,1]{3,1,2,0:T(8,128)S(1)} %get-tuple-element.30), channel_id=1, source_target_pairs={{1,0},{2,1},{3,2},{5,4},{6,5},{7,6},{9,8},{10,9},{11,10},{13,12},{... | collective-permute-start | bytes 3272 | tf_op jit(solution)/shard_map/ppermute | solution.py:21
Sparse Core Ops, SparseCore 0:
  143.0 39.9 all-reduce.5
where the time goes:
time: 274 us; the launch traced here: 272 us
  waiting for transfers between devices  87.1 us (32%)
  starting transfers between devices  85.8 us (31%)
  other arithmetic  55.4 us (20%)
  local copies, waits for them, and re-layouts  27.6 us (10%)
  between operations  14.6 us (5%)
    ppermute x14, starting transfers between devices, with_halo(): before = lax.ppermute(last, axis, up)  54.2 us
    ppermute x14, waiting for transfers between devices, with_halo(): after = lax.ppermute(initial, axis, down)  44.2 us
    psum x1, waiting for transfers between devices, on_device(): conductivity = lax.psum(partial_cond, 'grp')  40 us
    ppermute x14, starting transfers between devices, with_halo(): after = lax.ppermute(initial, axis, down)  31.6 us
    select_n x1, other arithmetic, on_device(): jnp.where(active, field + tendency(section_halo(field), speeds), 0.0)  14.5 us
    mul x1, other arithmetic, on_device(): sigma = ARCHIE * jnp.exp(advanced) * poro * poro * water * water  11.8 us
    reduce_sum x1, other arithmetic, on_device(): coarse = sigma.reshape(layers, coarse_x, 2, coarse_y, 2).sum(axis=(2, 4))  9.53 us
    mul x1, local copies, waits for them, and re-layouts, on_device(): sigma = ARCHIE * jnp.exp(advanced) * poro * poro * water * water  6.37 us
  transfers between devices with their start and end apart: 29, of which 14 were waited for; matrix products, arithmetic and copies ran while one was open for 28% of the time, Pallas kernels for 0%

commit v1 on v0

--- a/solution.py
+++ b/solution.py
@@ -111,7 +111,7 @@
     partial_cond = jnp.dot(
         weights, coarse.reshape(layers, coarse_x * coarse_y), precision=lax.Precision.HIGHEST
     ).reshape(resist_layers, coarse_x, coarse_y)
-    conductivity = lax.psum(partial_cond, "grp")
+    conductivity = jnp.sum(lax.all_gather(partial_cond, "grp"), axis=0)
     grid_x = coarse_x * lax.axis_size("gx")
     grid_y = coarse_y * lax.axis_size("gy")
     potential = lax.dynamic_slice_in_dim(init_potential, group_index, 1, 0)

time: 274 us -> 217 us (0.79)
  waiting for transfers between devices: 87.1 us -> 43.3 us
  between operations: 14.6 us -> 1.27 us
  blocking collectives: 0 us -> 6.51 us
  other arithmetic: 55.4 us -> 51.9 us
    psum x1 -> x0, waiting for transfers between devices: 40 us -> none  [on_device(): conductivity = lax.psum(partial_cond, 'grp')]
    all_gather x0 -> x1, blocking collectives: none -> 6.51 us  [on_device(): conductivity = jnp.sum(lax.all_gather(partial_cond, 'grp'), axis=0)]
    ppermute x14, waiting for transfers between devices: 44.2 us -> 40.5 us  [with_halo(): after = lax.ppermute(initial, axis, down)]
    slice x11 -> x10, local copies, waits for them, and re-layouts: 5.82 us -> 5.73 us  [with_halo(): last = lax.slice_in_dim(shard, length - width, length, axis=dim)]
  transfers between devices with their start and end apart: 29 -> 28, of which waited for: 14 -> 13; matrix products, arithmetic and copies ran while one was open for 28% -> 18% of each run, Pallas kernels for 0% -> 0%
where the time goes in v1:
time: 217 us; the launch traced here: 213 us
  starting transfers between devices  84.4 us (39%)
  other arithmetic  51.9 us (24%)
  waiting for transfers between devices  43.3 us (20%)
  local copies, waits for them, and re-layouts  25.6 us (12%)
  blocking collectives  6.51 us (3%)
    ppermute x14, starting transfers between devices, with_halo(): before = lax.ppermute(last, axis, up)  53 us
    ppermute x14, waiting for transfers between devices, with_halo(): after = lax.ppermute(initial, axis, down)  40.5 us
    ppermute x14, starting transfers between devices, with_halo(): after = lax.ppermute(initial, axis, down)  31.3 us
    select_n x1, other arithmetic, on_device(): jnp.where(active, field + tendency(section_halo(field), speeds), 0.0)  14.1 us
    mul x1, other arithmetic, on_device(): sigma = ARCHIE * jnp.exp(advanced) * poro * poro * water * water  11.9 us
    reduce_sum x1, other arithmetic, on_device(): coarse = sigma.reshape(layers, coarse_x, 2, coarse_y, 2).sum(axis=(2, 4))  9.53 us
    all_gather x1, blocking collectives, on_device(): conductivity = jnp.sum(lax.all_gather(partial_cond, 'grp'), axis=0)  6.51 us
    mul x1, local copies, waits for them, and re-layouts, on_device(): sigma = ARCHIE * jnp.exp(advanced) * poro * poro * water * water  6.36 us
  transfers between devices with their start and end apart: 28, of which 13 were waited for; matrix products, arithmetic and copies ran while one was open for 18% of the time, Pallas kernels for 0%

profile of v1, /device:TPU:70, one launch (start us, length us, event | category | flops | bytes accessed | tf_op | source)
XLA Modules:
  0.0 213.3 jit_solution(1642394528583420335)
XLA Ops:
  0.7 1.8 broadcast_select_fusion
  2.5 1.9 collective-permute-start
  4.4 3.6 %collective-permute-start.1 = (f32[1,64,256]{2,1,0:T(8,128)S(1)}, f32[1,64,256]{2,1,0:T(8,128)S(1)}, u32[]{:S(2)}, u32[]{:S(2)}) collective-permute-start(f32[1,64,256]{2,1,0:T(8,128)S(1)} %get-tuple-element.22), channel_id=1, source_target_pairs={{64,0},{128,64},{192,128},{65,1},{129,65},{193,129},{66,2},{130,66... | collective-permute-start | bytes 196616 | tf_op jit(solution)/shard_map/ppermute | solution.py:21
  8.2 4.7 %collective-permute-start.16 = (f32[1,8,1,128]{3,1,2,0:T(8,128)S(1)}, f32[1,8,1,128]{3,1,2,0:T(8,128)S(1)}, u32[]{:S(2)}, u32[]{:S(2)}) collective-permute-start(f32[1,8,1,128]{3,1,2,0:T(8,128)S(1)} %get-tuple-element.38), channel_id=1, source_target_pairs={{0,4},{4,8},{8,12},{12,16},{16,20},{20,24},{24,28},{28,32},{32,36}... | collective-permute-start | bytes 12296 | tf_op jit(solution)/shard_map/ppermute | solution.py:20
  12.9 2.7 %collective-permute-start.17 = (f32[1,8,1,128]{3,1,2,0:T(8,128)S(1)}, f32[1,8,1,128]{3,1,2,0:T(8,128)S(1)}, u32[]{:S(2)}, u32[]{:S(2)}) collective-permute-start(f32[1,8,1,128]{3,1,2,0:T(8,128)S(1)} %get-tuple-element.37), channel_id=1, source_target_pairs={{4,0},{8,4},{12,8},{16,12},{20,16},{24,20},{28,24},{32,28},{36,32}... | collective-permute-start | bytes 12296 | tf_op jit(solution)/shard_map/ppermute | solution.py:21
  15.6 1.8 fusion.129
  18.6 5.6 %collective-permute-start.2 = (f32[34,1,256]{2,1,0:T(1,128)S(1)}, f32[34,1,256]{2,1,0:T(1,128)S(1)}, u32[]{:S(2)}, u32[]{:S(2)}) collective-permute-start(f32[34,1,256]{2,1,0:T(1,128)S(1)} %get-tuple-element.17), channel_id=1, source_target_pairs={{0,4},{4,8},{8,12},{12,16},{16,20},{20,24},{24,28},{28,32},{32,36}... | collective-permute-start | bytes 104456 | tf_op jit(solution)/shard_map/ppermute | solution.py:20
  24.2 1.9 collective-permute-start.3
  26.1 6.3 %collective-permute-done.3 = f32[34,1,256]{2,1,0:T(1,128)S(1)} collective-permute-done((f32[34,1,256]{2,1,0:T(1,128)S(1)}, f32[34,1,256]{2,1,0:T(1,128)S(1)}, u32[]{:S(2)}, u32[]{:S(2)}) %collective-permute-start.3) | collective-permute-done | bytes 34848 | tf_op jit(solution)/shard_map/ppermute | solution.py:21
  32.8 1.9 fusion.118
  34.6 1.8 copy.23
  36.4 3.5 %collective-permute-start.4 = (f32[34,66,1]{1,2,0:T(1,128)S(1)}, f32[34,66,1]{1,2,0:T(1,128)S(1)}, u32[]{:S(2)}, u32[]{:S(2)}) collective-permute-start(f32[34,66,1]{1,2,0:T(1,128)S(1)} %copy.23), channel_id=1, source_target_pairs={{0,1},{1,2},{2,3},{4,5},{5,6},{6,7},{8,9},{9,10},{10,11},{12,13},{... | collective-permute-start | bytes 26936 | tf_op jit(solution)/shard_map/ppermute | solution.py:20
  41.7 5.4 %convert_element_type.64 = f32[3,1,32,64,256]{4,3,2,1,0:T(8,128)} convert(bf16[3,1,32,64,256]{4,3,2,1,0:T(8,128)(2,1)} %param.8) | non-fusion elementwise | flops 1572864 | bytes 9437184 | tf_op jit(solution)/shard_map/convert_element_type | solution.py:92
  48.7 1.6 copy.26
  50.3 14.1 %fusion.31 = f32[32,64,256]{2,1,0:T(8,128)S(1)} fusion(f32[32,64,256]{2,1,0:T(8,128)} %copy-done.1, f32[34,1,256]{2,1,0:T(1,128)S(1)} %collective-permute-done.3, f32[1,64,256]{2,1,0:T(8,128)S(1)} %collective-permute-done.1, f32[1,64,256]{2,1,0:T(8,128)S(1)} %collective-permute-done, f32[34,1,256]{2,1,0:T(1,128)S(1)} %collective-permute-done.2, ...), kind=kLoop, calls=%fused_computation.66 | loop fusion | flops 28311552 | bytes 10704417 | tf_op jit(solution)/shard_map/jit(_where)/select_n | solution.py:94
  64.5 1.9 collective-permute-start.6
  66.4 3.6 %collective-permute-start.7 = (f32[1,64,256]{2,1,0:T(8,128)S(1)}, f32[1,64,256]{2,1,0:T(8,128)S(1)}, u32[]{:S(2)}, u32[]{:S(2)}) collective-permute-start(f32[1,64,256]{2,1,0:T(8,128)S(1)} %get-tuple-element.20), channel_id=1, source_target_pairs={{64,0},{128,64},{192,128},{65,1},{129,65},{193,129},{66,2},{130,66... | collective-permute-start | bytes 196616 | tf_op jit(solution)/shard_map/ppermute | solution.py:21
  70.1 1.9 collective-permute-done.7
  72.0 4.8 %collective-permute-start.8 = (f32[34,1,256]{2,1,0:T(1,128)S(1)}, f32[34,1,256]{2,1,0:T(1,128)S(1)}, u32[]{:S(2)}, u32[]{:S(2)}) collective-permute-start(f32[34,1,256]{2,1,0:T(1,128)S(1)} %get-tuple-element.15), channel_id=1, source_target_pairs={{0,4},{4,8},{8,12},{12,16},{16,20},{20,24},{24,28},{28,32},{32,36}... | collective-permute-start | bytes 104456 | tf_op jit(solution)/shard_map/ppermute | solution.py:20
  76.8 2.5 %collective-permute-start.9 = (f32[34,1,256]{2,1,0:T(1,128)S(1)}, f32[34,1,256]{2,1,0:T(1,128)S(1)}, u32[]{:S(2)}, u32[]{:S(2)}) collective-permute-start(f32[34,1,256]{2,1,0:T(1,128)S(1)} %get-tuple-element.16), channel_id=1, source_target_pairs={{4,0},{8,4},{12,8},{16,12},{20,16},{24,20},{28,24},{32,28},{36,32}... | collective-permute-start | bytes 104456 | tf_op jit(solution)/shard_map/ppermute | solution.py:21
  79.5 6.8 %collective-permute-done.9 = f32[34,1,256]{2,1,0:T(1,128)S(1)} collective-permute-done((f32[34,1,256]{2,1,0:T(1,128)S(1)}, f32[34,1,256]{2,1,0:T(1,128)S(1)}, u32[]{:S(2)}, u32[]{:S(2)}) %collective-permute-start.9) | collective-permute-done | bytes 34848 | tf_op jit(solution)/shard_map/ppermute | solution.py:21
  86.6 1.8 fusion.117
  88.4 1.7 copy.27
  90.1 4.6 %collective-permute-start.10 = (f32[34,66,1]{1,2,0:T(1,128)S(1)}, f32[34,66,1]{1,2,0:T(1,128)S(1)}, u32[]{:S(2)}, u32[]{:S(2)}) collective-permute-start(f32[34,66,1]{1,2,0:T(1,128)S(1)} %copy.27), channel_id=1, source_target_pairs={{0,1},{1,2},{2,3},{4,5},{5,6},{6,7},{8,9},{9,10},{10,11},{12,13},{... | collective-permute-start | bytes 26936 | tf_op jit(solution)/shard_map/ppermute | solution.py:20
  94.7 1.7 copy.29
  99.5 2.6 %collective-permute-done.11 = f32[34,66,1]{1,2,0:T(1,128)S(1)} collective-permute-done((f32[34,66,1]{1,2,0:T(1,128)S(1)}, f32[34,66,1]{1,2,0:T(1,128)S(1)}, u32[]{:S(2)}, u32[]{:S(2)}) %collective-permute-start.11) | collective-permute-done | bytes 9008 | tf_op jit(solution)/shard_map/ppermute | solution.py:21
  103.7 11.9 %multiply_multiply_fusion = (f32[32,64,256]{2,1,0:T(8,128)}, f32[32,64,256]{2,1,0:T(8,128)}) fusion(bf16[1,32,64,256]{3,2,1,0:T(8,128)(2,1)} %param.10, bf16[1,32,64,256]{3,2,1,0:T(8,128)(2,1)} %param.9, f32[32,64,256]{2,1,0:T(8,128)S(1)} %fusion.31, f32[3,1,32,64,256]{4,3,2,1,0:T(8,128)} %convert_element_type.64, f32[34,66,1]{2,1,0:T(8,128)} %copy.30, ...), kind=kLoop, calls=%fused_computation | loop fusion | flops 33554432 | bytes 16996896 | tf_op jit(solution)/shard_map/mul | solution.py:99
  115.5 6.4 %copy.31 = f32[32,64,256]{0,2,1:T(8,128)} copy(f32[32,64,256]{2,1,0:T(8,128)} %get-tuple-element.9) | data formatting | bytes 4194304 | tf_op jit(solution)/shard_map/mul | solution.py:99
  121.9 9.5 %reduce_sum.18 = f32[32,32,128]{0,2,1:T(8,128)S(1)} reduce(f32[32,32,2,128,2]{0,4,3,2,1:T(2,128)} %bitcast.110, f32[]{:T(128)} %constant.8.clone.1), dimensions={2,4}, to_apply=%region_1.2 | reduce | flops 393216 | bytes 2621444 | tf_op jit(solution)/shard_map/reduce_sum | solution.py:102
  132.4 6.5 %all-gather = f32[32,32,128]{2,0,1:T(8,128)S(1)} all-gather(f32[8,32,128]{2,0,1:T(8,128)S(1)} %fusion.49), channel_id=2, replica_groups=mesh['grp'=4,'gx'=16,'gy'=4] {'grp'}, dimensions={0}, use_global_device_ids=true | all-gather | bytes 655360 | tf_op jit(solution)/shard_map/all_gather | solution.py:114
  139.0 5.4 %collective-permute-start.12 = (f32[8,1,128]{2,0,1:T(8,128)S(1)}, f32[8,1,128]{2,0,1:T(8,128)S(1)}, u32[]{:S(2)}, u32[]{:S(2)}) collective-permute-start(f32[8,1,128]{2,0,1:T(8,128)S(1)} %get-tuple-element.36), channel_id=1, source_target_pairs={{0,4},{4,8},{8,12},{12,16},{16,20},{20,24},{24,28},{28,32},{32,36}... | collective-permute-start | bytes 12296 | tf_op jit(solution)/shard_map/ppermute | solution.py:20
  144.4 1.9 collective-permute-start.13
  146.4 3.5 %collective-permute-start.18 = (f32[1,8,34,1]{3,1,2,0:T(8,128)S(1)}, f32[1,8,34,1]{3,1,2,0:T(8,128)S(1)}, u32[]{:S(2)}, u32[]{:S(2)}) collective-permute-start(f32[1,8,34,1]{3,1,2,0:T(8,128)S(1)} %get-tuple-element.29), channel_id=1, source_target_pairs={{0,1},{1,2},{2,3},{4,5},{5,6},{6,7},{8,9},{9,10},{10,11},{12,13},{... | collective-permute-start | bytes 3272 | tf_op jit(solution)/shard_map/ppermute | solution.py:20
  152.4 3.5 %collective-permute-start.14 = (f32[8,34,1]{2,0,1:T(8,128)S(1)}, f32[8,34,1]{2,0,1:T(8,128)S(1)}, u32[]{:S(2)}, u32[]{:S(2)}) collective-permute-start(f32[8,34,1]{2,0,1:T(8,128)S(1)} %get-tuple-element.28), channel_id=1, source_target_pairs={{0,1},{1,2},{2,3},{4,5},{5,6},{6,7},{8,9},{9,10},{10,11},{12,13},{... | collective-permute-start | bytes 3272 | tf_op jit(solution)/shard_map/ppermute | solution.py:20
  158.5 4.4 %collective-permute-done.15 = f32[8,34,1]{2,0,1:T(8,128)S(1)} collective-permute-done((f32[8,34,1]{2,0,1:T(8,128)S(1)}, f32[8,34,1]{2,0,1:T(8,128)S(1)}, u32[]{:S(2)}, u32[]{:S(2)}) %collective-permute-start.15) | collective-permute-done | bytes 1120 | tf_op jit(solution)/shard_map/ppermute | solution.py:21
  163.2 1.7 fusion.86
  164.9 6.3 %collective-permute-start.20 = (f32[1,8,1,128]{3,1,2,0:T(8,128)S(1)}, f32[1,8,1,128]{3,1,2,0:T(8,128)S(1)}, u32[]{:S(2)}, u32[]{:S(2)}) collective-permute-start(f32[1,8,1,128]{3,1,2,0:T(8,128)S(1)} %get-tuple-element.33), channel_id=1, source_target_pairs={{0,4},{4,8},{8,12},{12,16},{16,20},{20,24},{24,28},{28,32},{32,36}... | collective-permute-start | bytes 12296 | tf_op jit(solution)/shard_map/ppermute | solution.py:20
  171.3 1.9 collective-permute-start.21
  173.2 6.0 %collective-permute-done.21 = f32[1,8,1,128]{3,1,2,0:T(8,128)S(1)} collective-permute-done((f32[1,8,1,128]{3,1,2,0:T(8,128)S(1)}, f32[1,8,1,128]{3,1,2,0:T(8,128)S(1)}, u32[]{:S(2)}, u32[]{:S(2)}) %collective-permute-start.21) | collective-permute-done | bytes 4128 | tf_op jit(solution)/shard_map/ppermute | solution.py:21
  179.3 3.2 %collective-permute-start.22 = (f32[1,8,34,1]{3,1,2,0:T(8,128)S(1)}, f32[1,8,34,1]{3,1,2,0:T(8,128)S(1)}, u32[]{:S(2)}, u32[]{:S(2)}) collective-permute-start(f32[1,8,34,1]{3,1,2,0:T(8,128)S(1)} %get-tuple-element.25), channel_id=1, source_target_pairs={{0,1},{1,2},{2,3},{4,5},{5,6},{6,7},{8,9},{9,10},{10,11},{12,13},{... | collective-permute-start | bytes 3272 | tf_op jit(solution)/shard_map/ppermute | solution.py:20
  185.0 4.4 %collective-permute-done.23 = f32[1,8,34,1]{3,1,2,0:T(8,128)S(1)} collective-permute-done((f32[1,8,34,1]{3,1,2,0:T(8,128)S(1)}, f32[1,8,34,1]{3,1,2,0:T(8,128)S(1)}, u32[]{:S(2)}, u32[]{:S(2)}) %collective-permute-start.23) | collective-permute-done | bytes 1120 | tf_op jit(solution)/shard_map/ppermute | solution.py:21
  189.7 1.7 fusion.72
  191.4 2.2 %collective-permute-start.24 = (f32[1,8,1,128]{3,1,2,0:T(8,128)S(1)}, f32[1,8,1,128]{3,1,2,0:T(8,128)S(1)}, u32[]{:S(2)}, u32[]{:S(2)}) collective-permute-start(f32[1,8,1,128]{3,1,2,0:T(8,128)S(1)} %get-tuple-element.31), channel_id=1, source_target_pairs={{0,4},{4,8},{8,12},{12,16},{16,20},{20,24},{24,28},{28,32},{32,36}... | collective-permute-start | bytes 12296 | tf_op jit(solution)/shard_map/ppermute | solution.py:20
  193.7 5.1 %collective-permute-start.25 = (f32[1,8,1,128]{3,1,2,0:T(8,128)S(1)}, f32[1,8,1,128]{3,1,2,0:T(8,128)S(1)}, u32[]{:S(2)}, u32[]{:S(2)}) collective-permute-start(f32[1,8,1,128]{3,1,2,0:T(8,128)S(1)} %get-tuple-element.32), channel_id=1, source_target_pairs={{4,0},{8,4},{12,8},{16,12},{20,16},{24,20},{28,24},{32,28},{36,32}... | collective-permute-start | bytes 12296 | tf_op jit(solution)/shard_map/ppermute | solution.py:21
  198.8 2.8 %collective-permute-done.25 = f32[1,8,1,128]{3,1,2,0:T(8,128)S(1)} collective-permute-done((f32[1,8,1,128]{3,1,2,0:T(8,128)S(1)}, f32[1,8,1,128]{3,1,2,0:T(8,128)S(1)}, u32[]{:S(2)}, u32[]{:S(2)}) %collective-permute-start.25) | collective-permute-done | bytes 4128 | tf_op jit(solution)/shard_map/ppermute | solution.py:21
  201.7 1.9 collective-permute-start.26
  206.2 4.4 %collective-permute-done.27 = f32[1,8,34,1]{3,1,2,0:T(8,128)S(1)} collective-permute-done((f32[1,8,34,1]{3,1,2,0:T(8,128)S(1)}, f32[1,8,34,1]{3,1,2,0:T(8,128)S(1)}, u32[]{:S(2)}, u32[]{:S(2)}) %collective-permute-start.27) | collective-permute-done | bytes 1120 | tf_op jit(solution)/shard_map/ppermute | solution.py:21
  210.9 1.7 fusion.58
  (80 shorter events, 23.1 us)
Async XLA Ops:
  0.6 7.4 %copy-start = (f32[4,8,32,128]{3,2,1,0:T(8,128)S(1)}, f32[4,8,32,128]{3,2,1,0:T(8,128)}, u32[]{:S(2)}) copy-start(f32[4,8,32,128]{3,2,1,0:T(8,128)} %param.13) | copy-start | bytes 1572868
  2.5 16.1 %collective-permute-start = (f32[1,64,256]{2,1,0:T(8,128)S(1)}, f32[1,64,256]{2,1,0:T(8,128)S(1)}, u32[]{:S(2)}, u32[]{:S(2)}) collective-permute-start(f32[1,64,256]{2,1,0:T(8,128)S(1)} %get-tuple-element.21), channel_id=1, source_target_pairs={{0,64},{64,128},{128,192},{1,65},{65,129},{129,193},{2,66},{66,130... | collective-permute-start | bytes 196616 | tf_op jit(solution)/shard_map/ppermute | solution.py:20
  4.4 14.2 %collective-permute-start.1 = (f32[1,64,256]{2,1,0:T(8,128)S(1)}, f32[1,64,256]{2,1,0:T(8,128)S(1)}, u32[]{:S(2)}, u32[]{:S(2)}) collective-permute-start(f32[1,64,256]{2,1,0:T(8,128)S(1)} %get-tuple-element.22), channel_id=1, source_target_pairs={{64,0},{128,64},{192,128},{65,1},{129,65},{193,129},{66,2},{130,66... | collective-permute-start | bytes 196616 | tf_op jit(solution)/shard_map/ppermute | solution.py:21
  8.2 61.9 %collective-permute-start.16 = (f32[1,8,1,128]{3,1,2,0:T(8,128)S(1)}, f32[1,8,1,128]{3,1,2,0:T(8,128)S(1)}, u32[]{:S(2)}, u32[]{:S(2)}) collective-permute-start(f32[1,8,1,128]{3,1,2,0:T(8,128)S(1)} %get-tuple-element.38), channel_id=1, source_target_pairs={{0,4},{4,8},{8,12},{12,16},{16,20},{20,24},{24,28},{28,32},{32,36}... | collective-permute-start | bytes 12296 | tf_op jit(solution)/shard_map/ppermute | solution.py:20
  12.9 4.5 %copy-start.4 = (s32[8]{0:T(128)S(1)}, s32[8]{0:T(128)}, u32[]{:S(2)}) copy-start(s32[8]{0:T(128)} %param.11) | copy-start | bytes 100
  12.9 4.7 %copy-start.3 = (s32[4,2]{0,1:T(2,128)S(1)}, s32[4,2]{0,1:T(2,128)}, u32[]{:S(2)}) copy-start(s32[4,2]{0,1:T(2,128)} %param.12) | copy-start | bytes 100
  12.9 85.1 %collective-permute-start.17 = (f32[1,8,1,128]{3,1,2,0:T(8,128)S(1)}, f32[1,8,1,128]{3,1,2,0:T(8,128)S(1)}, u32[]{:S(2)}, u32[]{:S(2)}) collective-permute-start(f32[1,8,1,128]{3,1,2,0:T(8,128)S(1)} %get-tuple-element.37), channel_id=1, source_target_pairs={{4,0},{8,4},{12,8},{16,12},{20,16},{24,20},{28,24},{32,28},{36,32}... | collective-permute-start | bytes 12296 | tf_op jit(solution)/shard_map/ppermute | solution.py:21
  17.3 15.4 %copy-start.1 = (f32[32,64,256]{2,1,0:T(8,128)}, f32[32,64,256]{2,1,0:T(8,128)S(1)}, u32[]{:S(2)}) copy-start(f32[32,64,256]{2,1,0:T(8,128)S(1)} %fusion.129) | copy-start | bytes 6291460
  18.6 7.5 %collective-permute-start.2 = (f32[34,1,256]{2,1,0:T(1,128)S(1)}, f32[34,1,256]{2,1,0:T(1,128)S(1)}, u32[]{:S(2)}, u32[]{:S(2)}) collective-permute-start(f32[34,1,256]{2,1,0:T(1,128)S(1)} %get-tuple-element.17), channel_id=1, source_target_pairs={{0,4},{4,8},{8,12},{12,16},{16,20},{20,24},{24,28},{28,32},{32,36}... | collective-permute-start | bytes 104456 | tf_op jit(solution)/shard_map/ppermute | solution.py:20
  24.2 8.2 %collective-permute-start.3 = (f32[34,1,256]{2,1,0:T(1,128)S(1)}, f32[34,1,256]{2,1,0:T(1,128)S(1)}, u32[]{:S(2)}, u32[]{:S(2)}) collective-permute-start(f32[34,1,256]{2,1,0:T(1,128)S(1)} %get-tuple-element.18), channel_id=1, source_target_pairs={{4,0},{8,4},{12,8},{16,12},{20,16},{24,20},{28,24},{32,28},{36,32}... | collective-permute-start | bytes 104456 | tf_op jit(solution)/shard_map/ppermute | solution.py:21
  34.6 5.3 %copy-start.2 = (f32[34,66,1]{2,1,0:T(8,128)S(1)}, f32[34,66,1]{2,1,0:T(8,128)}, u32[]{:S(2)}) copy-start(f32[34,66,1]{2,1,0:T(8,128)} %get-tuple-element.13) | copy-start | bytes 26932
  36.4 10.7 %collective-permute-start.4 = (f32[34,66,1]{1,2,0:T(1,128)S(1)}, f32[34,66,1]{1,2,0:T(1,128)S(1)}, u32[]{:S(2)}, u32[]{:S(2)}) collective-permute-start(f32[34,66,1]{1,2,0:T(1,128)S(1)} %copy.23), channel_id=1, source_target_pairs={{0,1},{1,2},{2,3},{4,5},{5,6},{6,7},{8,9},{9,10},{10,11},{12,13},{... | collective-permute-start | bytes 26936 | tf_op jit(solution)/shard_map/ppermute | solution.py:20
  40.4 8.3 %collective-permute-start.5 = (f32[34,66,1]{1,2,0:T(1,128)S(1)}, f32[34,66,1]{1,2,0:T(1,128)S(1)}, u32[]{:S(2)}, u32[]{:S(2)}) collective-permute-start(f32[34,66,1]{1,2,0:T(1,128)S(1)} %copy.25), channel_id=1, source_target_pairs={{1,0},{2,1},{3,2},{5,4},{6,5},{7,6},{9,8},{10,9},{11,10},{13,12},{... | collective-permute-start | bytes 26936 | tf_op jit(solution)/shard_map/ppermute | solution.py:21
  64.5 5.6 %collective-permute-start.6 = (f32[1,64,256]{2,1,0:T(8,128)S(1)}, f32[1,64,256]{2,1,0:T(8,128)S(1)}, u32[]{:S(2)}, u32[]{:S(2)}) collective-permute-start(f32[1,64,256]{2,1,0:T(8,128)S(1)} %get-tuple-element.19), channel_id=1, source_target_pairs={{0,64},{64,128},{128,192},{1,65},{65,129},{129,193},{2,66},{66,130... | collective-permute-start | bytes 196616 | tf_op jit(solution)/shard_map/ppermute | solution.py:20
  66.4 5.5 %collective-permute-start.7 = (f32[1,64,256]{2,1,0:T(8,128)S(1)}, f32[1,64,256]{2,1,0:T(8,128)S(1)}, u32[]{:S(2)}, u32[]{:S(2)}) collective-permute-start(f32[1,64,256]{2,1,0:T(8,128)S(1)} %get-tuple-element.20), channel_id=1, source_target_pairs={{64,0},{128,64},{192,128},{65,1},{129,65},{193,129},{66,2},{130,66... | collective-permute-start | bytes 196616 | tf_op jit(solution)/shard_map/ppermute | solution.py:21
  72.0 7.5 %collective-permute-start.8 = (f32[34,1,256]{2,1,0:T(1,128)S(1)}, f32[34,1,256]{2,1,0:T(1,128)S(1)}, u32[]{:S(2)}, u32[]{:S(2)}) collective-permute-start(f32[34,1,256]{2,1,0:T(1,128)S(1)} %get-tuple-element.15), channel_id=1, source_target_pairs={{0,4},{4,8},{8,12},{12,16},{16,20},{20,24},{24,28},{28,32},{32,36}... | collective-permute-start | bytes 104456 | tf_op jit(solution)/shard_map/ppermute | solution.py:20
  76.8 9.4 %collective-permute-start.9 = (f32[34,1,256]{2,1,0:T(1,128)S(1)}, f32[34,1,256]{2,1,0:T(1,128)S(1)}, u32[]{:S(2)}, u32[]{:S(2)}) collective-permute-start(f32[34,1,256]{2,1,0:T(1,128)S(1)} %get-tuple-element.16), channel_id=1, source_target_pairs={{4,0},{8,4},{12,8},{16,12},{20,16},{24,20},{28,24},{32,28},{36,32}... | collective-permute-start | bytes 104456 | tf_op jit(solution)/shard_map/ppermute | solution.py:21
  90.1 7.8 %collective-permute-start.10 = (f32[34,66,1]{1,2,0:T(1,128)S(1)}, f32[34,66,1]{1,2,0:T(1,128)S(1)}, u32[]{:S(2)}, u32[]{:S(2)}) collective-permute-start(f32[34,66,1]{1,2,0:T(1,128)S(1)} %copy.27), channel_id=1, source_target_pairs={{0,1},{1,2},{2,3},{4,5},{5,6},{6,7},{8,9},{9,10},{10,11},{12,13},{... | collective-permute-start | bytes 26936 | tf_op jit(solution)/shard_map/ppermute | solution.py:20
  96.5 5.7 %collective-permute-start.11 = (f32[34,66,1]{1,2,0:T(1,128)S(1)}, f32[34,66,1]{1,2,0:T(1,128)S(1)}, u32[]{:S(2)}, u32[]{:S(2)}) collective-permute-start(f32[34,66,1]{1,2,0:T(1,128)S(1)} %copy.29), channel_id=1, source_target_pairs={{1,0},{2,1},{3,2},{5,4},{6,5},{7,6},{9,8},{10,9},{11,10},{13,12},{... | collective-permute-start | bytes 26936 | tf_op jit(solution)/shard_map/ppermute | solution.py:21
  139.0 12.3 %collective-permute-start.12 = (f32[8,1,128]{2,0,1:T(8,128)S(1)}, f32[8,1,128]{2,0,1:T(8,128)S(1)}, u32[]{:S(2)}, u32[]{:S(2)}) collective-permute-start(f32[8,1,128]{2,0,1:T(8,128)S(1)} %get-tuple-element.36), channel_id=1, source_target_pairs={{0,4},{4,8},{8,12},{12,16},{16,20},{20,24},{24,28},{28,32},{32,36}... | collective-permute-start | bytes 12296 | tf_op jit(solution)/shard_map/ppermute | solution.py:20
  144.4 7.9 %collective-permute-start.13 = (f32[8,1,128]{2,0,1:T(8,128)S(1)}, f32[8,1,128]{2,0,1:T(8,128)S(1)}, u32[]{:S(2)}, u32[]{:S(2)}) collective-permute-start(f32[8,1,128]{2,0,1:T(8,128)S(1)} %get-tuple-element.35), channel_id=1, source_target_pairs={{4,0},{8,4},{12,8},{16,12},{20,16},{24,20},{28,24},{32,28},{36,32}... | collective-permute-start | bytes 12296 | tf_op jit(solution)/shard_map/ppermute | solution.py:21
  146.4 10.8 %collective-permute-start.18 = (f32[1,8,34,1]{3,1,2,0:T(8,128)S(1)}, f32[1,8,34,1]{3,1,2,0:T(8,128)S(1)}, u32[]{:S(2)}, u32[]{:S(2)}) collective-permute-start(f32[1,8,34,1]{3,1,2,0:T(8,128)S(1)} %get-tuple-element.29), channel_id=1, source_target_pairs={{0,1},{1,2},{2,3},{4,5},{5,6},{6,7},{8,9},{9,10},{10,11},{12,13},{... | collective-permute-start | bytes 3272 | tf_op jit(solution)/shard_map/ppermute | solution.py:20
  149.9 7.3 %collective-permute-start.19 = (f32[1,8,34,1]{3,1,2,0:T(8,128)S(1)}, f32[1,8,34,1]{3,1,2,0:T(8,128)S(1)}, u32[]{:S(2)}, u32[]{:S(2)}) collective-permute-start(f32[1,8,34,1]{3,1,2,0:T(8,128)S(1)} %get-tuple-element.30), channel_id=1, source_target_pairs={{1,0},{2,1},{3,2},{5,4},{6,5},{7,6},{9,8},{10,9},{11,10},{13,12},{... | collective-permute-start | bytes 3272 | tf_op jit(solution)/shard_map/ppermute | solution.py:21
  152.4 6.1 %collective-permute-start.14 = (f32[8,34,1]{2,0,1:T(8,128)S(1)}, f32[8,34,1]{2,0,1:T(8,128)S(1)}, u32[]{:S(2)}, u32[]{:S(2)}) collective-permute-start(f32[8,34,1]{2,0,1:T(8,128)S(1)} %get-tuple-element.28), channel_id=1, source_target_pairs={{0,1},{1,2},{2,3},{4,5},{5,6},{6,7},{8,9},{9,10},{10,11},{12,13},{... | collective-permute-start | bytes 3272 | tf_op jit(solution)/shard_map/ppermute | solution.py:20
  155.9 6.9 %collective-permute-start.15 = (f32[8,34,1]{2,0,1:T(8,128)S(1)}, f32[8,34,1]{2,0,1:T(8,128)S(1)}, u32[]{:S(2)}, u32[]{:S(2)}) collective-permute-start(f32[8,34,1]{2,0,1:T(8,128)S(1)} %get-tuple-element.27), channel_id=1, source_target_pairs={{1,0},{2,1},{3,2},{5,4},{6,5},{7,6},{9,8},{10,9},{11,10},{13,12},{... | collective-permute-start | bytes 3272 | tf_op jit(solution)/shard_map/ppermute | solution.py:21
  164.9 8.3 %collective-permute-start.20 = (f32[1,8,1,128]{3,1,2,0:T(8,128)S(1)}, f32[1,8,1,128]{3,1,2,0:T(8,128)S(1)}, u32[]{:S(2)}, u32[]{:S(2)}) collective-permute-start(f32[1,8,1,128]{3,1,2,0:T(8,128)S(1)} %get-tuple-element.33), channel_id=1, source_target_pairs={{0,4},{4,8},{8,12},{12,16},{16,20},{20,24},{24,28},{28,32},{32,36}... | collective-permute-start | bytes 12296 | tf_op jit(solution)/shard_map/ppermute | solution.py:20
  171.3 7.9 %collective-permute-start.21 = (f32[1,8,1,128]{3,1,2,0:T(8,128)S(1)}, f32[1,8,1,128]{3,1,2,0:T(8,128)S(1)}, u32[]{:S(2)}, u32[]{:S(2)}) collective-permute-start(f32[1,8,1,128]{3,1,2,0:T(8,128)S(1)} %get-tuple-element.34), channel_id=1, source_target_pairs={{4,0},{8,4},{12,8},{16,12},{20,16},{24,20},{28,24},{32,28},{36,32}... | collective-permute-start | bytes 12296 | tf_op jit(solution)/shard_map/ppermute | solution.py:21
  179.3 5.8 %collective-permute-start.22 = (f32[1,8,34,1]{3,1,2,0:T(8,128)S(1)}, f32[1,8,34,1]{3,1,2,0:T(8,128)S(1)}, u32[]{:S(2)}, u32[]{:S(2)}) collective-permute-start(f32[1,8,34,1]{3,1,2,0:T(8,128)S(1)} %get-tuple-element.25), channel_id=1, source_target_pairs={{0,1},{1,2},{2,3},{4,5},{5,6},{6,7},{8,9},{9,10},{10,11},{12,13},{... | collective-permute-start | bytes 3272 | tf_op jit(solution)/shard_map/ppermute | solution.py:20
  182.5 6.9 %collective-permute-start.23 = (f32[1,8,34,1]{3,1,2,0:T(8,128)S(1)}, f32[1,8,34,1]{3,1,2,0:T(8,128)S(1)}, u32[]{:S(2)}, u32[]{:S(2)}) collective-permute-start(f32[1,8,34,1]{3,1,2,0:T(8,128)S(1)} %get-tuple-element.26), channel_id=1, source_target_pairs={{1,0},{2,1},{3,2},{5,4},{6,5},{7,6},{9,8},{10,9},{11,10},{13,12},{... | collective-permute-start | bytes 3272 | tf_op jit(solution)/shard_map/ppermute | solution.py:21
  191.4 7.4 %collective-permute-start.24 = (f32[1,8,1,128]{3,1,2,0:T(8,128)S(1)}, f32[1,8,1,128]{3,1,2,0:T(8,128)S(1)}, u32[]{:S(2)}, u32[]{:S(2)}) collective-permute-start(f32[1,8,1,128]{3,1,2,0:T(8,128)S(1)} %get-tuple-element.31), channel_id=1, source_target_pairs={{0,4},{4,8},{8,12},{12,16},{16,20},{20,24},{24,28},{28,32},{32,36}... | collective-permute-start | bytes 12296 | tf_op jit(solution)/shard_map/ppermute | solution.py:20
  193.7 7.9 %collective-permute-start.25 = (f32[1,8,1,128]{3,1,2,0:T(8,128)S(1)}, f32[1,8,1,128]{3,1,2,0:T(8,128)S(1)}, u32[]{:S(2)}, u32[]{:S(2)}) collective-permute-start(f32[1,8,1,128]{3,1,2,0:T(8,128)S(1)} %get-tuple-element.32), channel_id=1, source_target_pairs={{4,0},{8,4},{12,8},{16,12},{20,16},{24,20},{28,24},{32,28},{36,32}... | collective-permute-start | bytes 12296 | tf_op jit(solution)/shard_map/ppermute | solution.py:21
  201.7 4.5 %collective-permute-start.26 = (f32[1,8,34,1]{3,1,2,0:T(8,128)S(1)}, f32[1,8,34,1]{3,1,2,0:T(8,128)S(1)}, u32[]{:S(2)}, u32[]{:S(2)}) collective-permute-start(f32[1,8,34,1]{3,1,2,0:T(8,128)S(1)} %get-tuple-element.23), channel_id=1, source_target_pairs={{0,1},{1,2},{2,3},{4,5},{5,6},{6,7},{8,9},{9,10},{10,11},{12,13},{... | collective-permute-start | bytes 3272 | tf_op jit(solution)/shard_map/ppermute | solution.py:20
  203.7 6.9 %collective-permute-start.27 = (f32[1,8,34,1]{3,1,2,0:T(8,128)S(1)}, f32[1,8,34,1]{3,1,2,0:T(8,128)S(1)}, u32[]{:S(2)}, u32[]{:S(2)}) collective-permute-start(f32[1,8,34,1]{3,1,2,0:T(8,128)S(1)} %get-tuple-element.24), channel_id=1, source_target_pairs={{1,0},{2,1},{3,2},{5,4},{6,5},{7,6},{9,8},{10,9},{11,10},{13,12},{... | collective-permute-start | bytes 3272 | tf_op jit(solution)/shard_map/ppermute | solution.py:21
